TPU v7x, 512 devices: a whole 4x8x8 slice. The times are simulated.
512 devices in a mesh: kv: 16 (over z, core), ep: 32 (over x, y).
Axes of the slice: x: 4, y: 8, z: 8, core: 2. Of those that a mesh axis runs over, the one named last changes fastest.
Arguments:
- queries: bfloat16 [32, 64, 2048], P('ep'), may hold values from -12 to 12
- new_keys: bfloat16 [32, 64, 512], P('ep'), may hold values from -12 to 12
- new_values: bfloat16 [32, 64, 512], P('ep'), may hold values from -6 to 6
- cache_keys: bfloat16 [32, 64, 128, 512], P('ep', 'kv'), may hold values from -12 to 12
- cache_values: bfloat16 [32, 64, 128, 512], P('ep', 'kv'), may hold values from -10 to 10
- page_table: int32 [32, 64], P('ep'), may hold values from 0 to 63, each once within a row
- cached_len: int32 [32], P('ep'), may hold values from 1 to 8192, 65536 in all
- moe_rows: bfloat16 [1024, 4096], P('ep'), may hold values from -6 to 6
- expert_ids: int32 [1024, 2], P('ep'), may hold values from 0 to 7, all different within a row; in each aligned block of 32 rows (0 to 31, 32 to 63, ...) at most 16 rows name the same one
- gate_probs: float32 [1024, 2], P('ep'), may hold values from 0.1 to 0.9
- w_gate: bfloat16 [32, 4096, 2048], P('ep', None, 'kv'), may hold values from -0.09375 to 0.09375
- w_up: bfloat16 [32, 4096, 2048], P('ep', None, 'kv'), may hold values from -0.09375 to 0.09375
- w_down: bfloat16 [32, 2048, 4096], P('ep', 'kv'), may hold values from -0.09375 to 0.09375
Outputs:
- attn_out: bfloat16 [32, 64, 2048], P('ep')
- moe_out: bfloat16 [1024, 4096], P('ep', 'kv')
Inputs may be any that keep to these rules, and one draw needn't show every extreme that they name: `page_table`: each row is a permutation of the 64 slots of its request. `cached_len`: cached positions at or past a request's length hold no data. `expert_ids`: each row names 2 different experts; among the 32 rows of one ep index no expert is named more than 16 times, and this bound is reached.
All inputs are finite; a program needn't handle non-finite values. No bound on the sum of `cached_len` on one device may be relied on, other than what follows from the above.
Results may differ from a plain program's by a relative error of at most 0.0085.
Values may be sent and summed in bfloat16 or wider, within the bound.
No kernel may reach another device: no remote copies, remote signals or barrier semaphores. Data moves between devices by JAX's collectives and lax.ppermute only.
A program may use at most 128 MiB of HBM per device.

v0:
```python
import math
import jax
import jax.numpy as jnp
from jax import lax
from jax.sharding import PartitionSpec as P

HD = 128
EXPERTS = 8
TOP = 2
HQ = 16
KVH = 4
PAGE = 128
POOL_DEV = 4
CAP = 16
ROPE_BASE = 10000.0
MASKED = -1e30


def merged(part, axis, combine):
    gathered = jax.tree.map(lambda a: lax.all_gather(a, axis), part)

    def take(source):
        return jax.tree.map(lambda a: lax.dynamic_index_in_dim(a, source, 0, False), gathered)

    return lax.fori_loop(
        1, lax.axis_size(axis), lambda source, state: combine(state, take(source)), take(0)
    )


def rotary(values, positions):
    half_width = values.shape[-1] // 2
    indices = jnp.arange(half_width, dtype=jnp.float32)
    frequency = jnp.power(ROPE_BASE, -2.0 * indices / values.shape[-1])
    angles = positions.astype(jnp.float32)[:, None] * frequency[None, :]
    cosine = jnp.cos(angles)[:, None, :]
    sine_part = jnp.sin(angles)[:, None, :]
    lower_half = values[..., :half_width]
    upper_half = values[..., half_width:]
    return jnp.concatenate(
        [
            lower_half * cosine - upper_half * sine_part,
            upper_half * cosine + lower_half * sine_part,
        ],
        axis=-1,
    )


def combine_parts(first, second):
    high_first, total_first, blend_first = first
    high_second, total_second, blend_second = second
    highest = jnp.maximum(high_first, high_second)
    factor_first = jnp.exp(high_first - highest)
    factor_second = jnp.exp(high_second - highest)
    row_count, head_count = highest.shape
    blended = (
        blend_first.reshape(row_count, head_count, -1) * factor_first[..., None]
        + blend_second.reshape(row_count, head_count, -1) * factor_second[..., None]
    )
    return (
        highest,
        total_first * factor_first + total_second * factor_second,
        blended.reshape(blend_first.shape),
    )


def on_device(
    queries,
    new_keys,
    new_values,
    cache_keys,
    cache_values,
    page_table,
    cached_len,
    moe_rows,
    expert_ids,
    gate_probs,
    w_gate,
    w_up,
    w_down,
):
    kv_index = lax.axis_index("kv")
    kv_count = lax.axis_size("kv")
    all_rows = queries.shape[1]
    block_rows = all_rows // kv_count
    length = cached_len[0]
    group_size = HQ // KVH
    score_scale = 1.0 / math.sqrt(HD)
    slot_ids = kv_index * POOL_DEV + jnp.arange(POOL_DEV, dtype=jnp.int32)
    matches = (page_table[0][:, None] == slot_ids[None, :]).astype(jnp.int32)
    page_index = jnp.sum(
        matches * jnp.arange(page_table.shape[1], dtype=jnp.int32)[:, None], axis=0
    )
    cached_pos = (page_index[:, None] * PAGE + jnp.arange(PAGE, dtype=jnp.int32)[None, :]).reshape(
        -1
    )
    block_start = kv_index * block_rows
    own_pos = length + block_start + jnp.arange(block_rows, dtype=jnp.int32)
    key_block = lax.dynamic_slice_in_dim(new_keys[0], block_start, block_rows, 0)
    value_block = lax.dynamic_slice_in_dim(new_values[0], block_start, block_rows, 0)
    own_keys = rotary(key_block.astype(jnp.float32).reshape(block_rows, KVH, HD), own_pos).astype(
        jnp.bfloat16
    )
    local_keys = jnp.concatenate([cache_keys[0].reshape(-1, KVH, HD), own_keys], axis=0)
    local_values = jnp.concatenate(
        [cache_values[0].reshape(-1, KVH, HD), value_block.reshape(block_rows, KVH, HD)], axis=0
    )
    key_pos = jnp.concatenate([cached_pos, own_pos])
    live_keys = jnp.concatenate([cached_pos < length, jnp.ones((block_rows,), jnp.bool_)])
    positions = length + jnp.arange(all_rows, dtype=jnp.int32)
    rotated = rotary(queries[0].astype(jnp.float32).reshape(all_rows, HQ, HD), positions).astype(
        jnp.bfloat16
    )
    grouped = rotated.reshape(all_rows, KVH, group_size, HD)
    scores = (
        jnp.einsum("nkgd,mkd->nkgm", grouped, local_keys, preferred_element_type=jnp.float32)
        * score_scale
    )
    usable = (live_keys[None, :] & (key_pos[None, :] <= positions[:, None]))[:, None, None, :]
    scores = jnp.where(usable, scores, MASKED)
    part_high = jnp.max(scores, axis=-1)
    weights = jnp.where(usable, jnp.exp(scores - part_high[..., None]), 0.0)
    part_total = jnp.sum(weights, axis=-1)
    part_blend = jnp.einsum(
        "nkgm,mkd->nkgd",
        weights.astype(jnp.bfloat16),
        local_values,
        preferred_element_type=jnp.float32,
    )
    partials = (
        part_high.reshape(all_rows, HQ),
        part_total.reshape(all_rows, HQ),
        part_blend.reshape(all_rows, HQ * HD),
    )
    highest, row_total, blended = merged(partials, "kv", combine_parts)
    attn_out = (
        (blended.reshape(all_rows, HQ, HD) / row_total[..., None])
        .reshape(1, all_rows, HQ * HD)
        .astype(jnp.bfloat16)
    )
    ep_count = lax.axis_size("ep")
    share_count = ep_count // EXPERTS
    tok_rows = moe_rows.shape[0]
    slot_total = ep_count * CAP
    flat_ids = expert_ids.reshape(-1)
    one_hot = (flat_ids[:, None] == jnp.arange(EXPERTS, dtype=jnp.int32)[None, :]).astype(jnp.int32)
    earlier = jnp.cumsum(one_hot, axis=0) - one_hot
    slot_rank = jnp.sum(earlier * one_hot, axis=1)
    slot_index = jnp.arange(slot_total, dtype=jnp.int32)
    dest_expert = slot_index // CAP // share_count
    dest_slot = slot_index % CAP
    matched = (flat_ids[None, :] == dest_expert[:, None]) & (
        slot_rank[None, :] == dest_slot[:, None]
    )
    select = jnp.sum(matched.astype(jnp.float32).reshape(slot_total, tok_rows, TOP), axis=2).astype(
        jnp.bfloat16
    )
    weight_map = jnp.sum(
        jnp.where(matched, gate_probs.reshape(-1)[None, :], 0.0).reshape(slot_total, tok_rows, TOP),
        axis=2,
    )
    outgoing = (
        jnp.dot(select, moe_rows, preferred_element_type=jnp.float32)
        .astype(jnp.bfloat16)
        .reshape(ep_count, CAP, -1)
    )
    arrived = lax.all_to_all(outgoing, "ep", split_axis=0, concat_axis=0, tiled=True).reshape(
        slot_total, -1
    )
    gate_proj = jnp.dot(arrived, w_gate[0], preferred_element_type=jnp.float32)
    up_proj = jnp.dot(arrived, w_up[0], preferred_element_type=jnp.float32)
    hidden = (jax.nn.silu(gate_proj) * up_proj).astype(jnp.bfloat16)
    out_width = w_down.shape[2] // kv_count
    down_split = w_down[0].reshape(w_down.shape[1], kv_count, out_width)
    down_cols = lax.all_to_all(down_split, "kv", split_axis=1, concat_axis=0, tiled=True).reshape(
        -1, out_width
    )
    summed = jnp.dot(
        lax.all_gather(hidden, "kv", axis=1, tiled=True),
        down_cols,
        preferred_element_type=jnp.float32,
    )
    returned = (
        lax.all_to_all(
            summed.reshape(ep_count, CAP, -1).astype(jnp.bfloat16),
            "ep",
            split_axis=0,
            concat_axis=0,
            tiled=True,
        )
        .astype(jnp.float32)
        .reshape(slot_total, -1)
    )
    moe_out = jnp.dot(
        weight_map.T, returned, precision=lax.Precision.HIGHEST, preferred_element_type=jnp.float32
    ).astype(jnp.bfloat16)
    return (attn_out, moe_out)


def solution(mesh):
    return jax.shard_map(
        on_device,
        mesh=mesh,
        in_specs=(
            P("ep", None, None),
            P("ep", None, None),
            P("ep", None, None),
            P("ep", "kv", None, None),
            P("ep", "kv", None, None),
            P("ep", None),
            P("ep"),
            P("ep", None),
            P("ep", None),
            P("ep", None),
            P("ep", None, "kv"),
            P("ep", None, "kv"),
            P("ep", "kv", None),
        ),
        out_specs=(P("ep", None, None), P("ep", "kv")),
        check_vma=False,
    )
```

profile of v0, /device:TPU:1, one launch (start us, length us, event | category | flops | bytes accessed | tf_op | source)
XLA Modules:
  0.0 284.0 jit_solution(5398753687239622973)
XLA Ops:
  7.2 0.8 copy.56
  8.7 0.8 convert_reduce_fusion
  9.6 2.2 convolution_convert_fusion
  11.8 102.2 %all_to_all.25 = bf16[32,16,4096]{2,1,0:T(8,128)(2,1)S(1)} all-to-all(bf16[32,16,4096]{2,1,0:T(8,128)(2,1)S(1)} %bitcast.135), channel_id=1, replica_groups=mesh['kv'=16,'ep'=32] {'ep'}, dimensions={0} | all-to-all | bytes 8388608 | tf_op jit(solution)/shard_map/all_to_all | solution.py:166
  113.9 1.3 fusion.14
  115.2 1.9 fusion.12
  118.2 0.9 copy.50
  119.7 0.7 bitcast_convert_fusion
  120.7 0.2 multiply_cosine_fusion
  120.9 0.2 fusion.50
  121.1 0.3 subtract_convert_fusion
  121.5 0.8 fusion.3
  122.3 0.8 fusion.9
  123.0 0.8 copy-done.1
  123.8 0.3 copy.54
  124.2 1.0 all_gather_reshape.11
  125.2 0.2 copy.67
  125.5 1.3 copy.58
  126.8 15.6 %all-to-all-start.1 = ((bf16[128,16,256]{2,0,1:T(8,128)(2,1)}), bf16[128,16,256]{2,0,1:T(8,128)(2,1)S(1)}, u32[]{:S(2)}, u32[]{:S(2)}) async-start(bf16[128,16,256]{2,0,1:T(8,128)(2,1)} %copy.58), calls=%async_computation.1 | async-start | bytes 2097152 | tf_op jit(solution)/shard_map/all_to_all | solution.py:174
  142.3 2.6 fusion.5
  145.0 28.9 %all-to-all-done.1 = bf16[128,16,256]{2,0,1:T(8,128)(2,1)S(1)} async-done(((bf16[128,16,256]{2,0,1:T(8,128)(2,1)}), bf16[128,16,256]{2,0,1:T(8,128)(2,1)S(1)}, u32[]{:S(2)}, u32[]{:S(2)}) %all-to-all-start.1) | async-done | bytes 1048608 | tf_op jit(solution)/shard_map/all_to_all | solution.py:174
  173.9 6.0 %all-gather.5.cloned.1.call-done = bf16[512,2048]{1,0:T(8,128)(2,1)} async-done(((bf16[512,128]{1,0:T(8,128)(2,1)}), bf16[512,2048]{1,0:T(8,128)(2,1)}) %all-gather.5.cloned.1.call-update) | async-done | bytes 2097168 | tf_op jit(solution)/shard_map/all_gather | solution.py:178
  179.9 3.0 %convolution_convert_fusion.1 = bf16[32,16,256]{2,1,0:T(8,128)(2,1)} fusion(bf16[32,16,2048]{2,1,0:T(8,128)(2,1)} %bitcast.146, bf16[2048,256,1]{1,0,2:T(8,128)(2,1)S(1)} %bitcast.140), kind=kOutput, calls=%fused_computation.18 | convolution fusion | flops 537001984 | bytes 3407872 | tf_op jit(solution)/shard_map/dot_general | solution.py:177
  182.9 10.4 %all-to-all-start.2 = ((bf16[32,16,256]{2,1,0:T(8,128)(2,1)}), bf16[32,16,256]{2,1,0:T(8,128)(2,1)S(1)}, u32[]{:S(2)}, u32[]{:S(2)}) async-start(bf16[32,16,256]{2,1,0:T(8,128)(2,1)} %convolution_convert_fusion.1), calls=%async_computation.2 | async-start | bytes 524288 | tf_op jit(solution)/shard_map/all_to_all | solution.py:183
  193.4 18.7 %all_gather.12 = f32[16,64,16]{1,2,0:T(8,128)S(1)} all-gather(f32[1,64,16]{1,2,0:T(8,128)S(1)} %bitcast.144), channel_id=1, replica_groups=mesh['kv'=16,'ep'=32] {'kv'}, dimensions={0}, use_global_device_ids=true | all-gather | bytes 69632 | tf_op jit(solution)/shard_map/all_gather | solution.py:20
  212.1 15.8 %all_gather.13 = f32[16,64,16]{1,2,0:T(8,128)S(1)} all-gather(f32[1,64,16]{1,2,0:T(8,128)S(1)} %bitcast.145), channel_id=1, replica_groups=mesh['kv'=16,'ep'=32] {'kv'}, dimensions={0}, use_global_device_ids=true | all-gather | bytes 69632 | tf_op jit(solution)/shard_map/all_gather | solution.py:20
  227.9 0.9 convolution_convert_fusion.2
  228.8 13.1 %all-gather.3.cloned.1.call-done = f32[16,64,2048]{2,1,0:T(8,128)} async-done(((f32[1,64,2048]{2,1,0:T(8,128)}), f32[16,64,2048]{2,1,0:T(8,128)}) %all-gather.3.cloned.1.call-update) | async-done | bytes 8388624 | tf_op jit(solution)/shard_map/all_gather | solution.py:20
  241.8 1.1 slice_bitcast_fusion
  242.9 33.0 %while.19 = (s32[]{:T(128)}, f32[64,16]{0,1:T(8,128)S(1)}, f32[64,16]{0,1:T(8,128)S(1)}, f32[64,2048]{1,0:T(8,128)S(1)}, f32[16,64,16]{1,2,0:T(8,128)S(1)}, /*in...) while((s32[]{:T(128)}, f32[64,16]{0,1:T(8,128)S(1)}, ...), condition=%wide.region_4.5_spmd, body=%wide.region_3.4_spmd.sunk | while | flops 399365 | bytes 3727511 | solution.py:25
  243.0 0.2 mul.308
  243.3 0.2 mul.309
  243.5 1.6 fusion.62
  245.2 0.2 mul.308
  245.5 0.2 mul.309
  245.7 1.6 fusion.62
  247.7 0.2 mul.309
  247.9 1.6 fusion.62
  249.9 0.2 mul.309
  250.1 1.6 fusion.62
  252.1 0.2 mul.309
  252.3 1.6 fusion.62
  254.3 0.2 mul.309
  254.5 1.6 fusion.62
  256.5 0.2 mul.309
  256.7 1.6 fusion.62
  258.7 0.2 mul.309
  258.9 1.6 fusion.62
  260.6 0.2 mul.308
  260.9 0.2 mul.309
  261.1 1.6 fusion.62
  263.1 0.2 mul.309
  263.3 1.6 fusion.62
  265.3 0.2 mul.309
  265.5 1.6 fusion.62
  267.5 0.2 mul.309
  267.7 1.6 fusion.62
  269.7 0.2 mul.309
  269.9 1.6 fusion.62
  271.9 0.2 mul.309
  272.1 1.6 fusion.62
  274.1 0.2 mul.309
  274.3 1.6 fusion.62
  276.2 0.9 fusion.27
  (108 shorter events, 7.3 us)
Async XLA Ops:
  7.2 106.8 %copy-start = (bf16[1,4096,128]{2,1,0:T(8,128)(2,1)S(1)}, bf16[1,4096,128]{2,1,0:T(8,128)(2,1)}, u32[]{:S(2)}) copy-start(bf16[1,4096,128]{2,1,0:T(8,128)(2,1)} %param.25) | copy-start | bytes 3145732
  7.2 172.8 %all-gather.5.cloned.1.call-start = ((), (), s32[]{:S(2)}) async-start(), calls=%async_computation.4 | async-start | bytes 2228224 | tf_op jit(solution)/shard_map/all_gather | solution.py:178
  113.9 1.3 copy-start.7
  115.2 2.7 copy-start.6
  115.2 2.9 %copy-start.3 = (bf16[1,4,128,512]{3,2,1,0:T(8,128)(2,1)S(1)}, bf16[1,4,128,512]{3,2,1,0:T(8,128)(2,1)}, u32[]{:S(2)}) copy-start(bf16[1,4,128,512]{3,2,1,0:T(8,128)(2,1)} %param.18) | copy-start | bytes 1572868
  117.1 1.9 copy-start.4
  117.2 124.7 %all-gather.3.cloned.1.call-start = ((), (), s32[]{:S(2)}) async-start(), calls=%async_computation.3 | async-start | bytes 8912896 | tf_op jit(solution)/shard_map/all_gather | solution.py:20
  118.0 1.3 copy-start.8
  119.2 2.3 copy-start.5
  122.3 1.6 copy-start.1
  123.8 1.4 copy-start.2
  126.8 47.1 %all-to-all-start.1 = ((bf16[128,16,256]{2,0,1:T(8,128)(2,1)}), bf16[128,16,256]{2,0,1:T(8,128)(2,1)S(1)}, u32[]{:S(2)}, u32[]{:S(2)}) async-start(bf16[128,16,256]{2,0,1:T(8,128)(2,1)} %copy.58), calls=%async_computation.1 | async-start | bytes 2097152 | tf_op jit(solution)/shard_map/all_to_all | solution.py:174
  182.9 45.0 %all-to-all-start.2 = ((bf16[32,16,256]{2,1,0:T(8,128)(2,1)}), bf16[32,16,256]{2,1,0:T(8,128)(2,1)S(1)}, u32[]{:S(2)}, u32[]{:S(2)}) async-start(bf16[32,16,256]{2,1,0:T(8,128)(2,1)} %convolution_convert_fusion.1), calls=%async_computation.2 | async-start | bytes 524288 | tf_op jit(solution)/shard_map/all_to_all | solution.py:183
Sparse Core Ops, SparseCore 0:
  117.3 62.6 all-gather.4
  182.1 59.7 all-gather.2
where the time goes:
time: 285 us; the launch traced here: 284 us
  blocking collectives  137 us (48%)
  waiting for transfers between devices  48.1 us (17%)
  other arithmetic  30.8 us (11%)
  starting transfers between devices  26.1 us (9%)
  local copies, waits for them, and re-layouts  16 us (6%)
  between operations  15 us (5%)
  matrix products  10.8 us (4%)
    all_to_all x1, blocking collectives, on_device(): lax.all_to_all(outgoing, 'ep', split_axis=0, concat_axis=0, tiled=True)  102 us
    all_gather x2, blocking collectives, merged(): gathered = jax.tree.map(lambda a: lax.all_gather(a, axis), part)  34.5 us
    all_to_all x1, waiting for transfers between devices, on_device(): lax.all_to_all(down_split, 'kv', split_axis=1, concat_axis=0, tiled=True)  28.9 us
    add x15, other arithmetic, combine_parts(): blend_first.reshape(row_count, head_count, -1) * factor_first[..., None]  23.9 us
    all_to_all x1, starting transfers between devices, on_device(): lax.all_to_all(down_split, 'kv', split_axis=1, concat_axis=0, tiled=True)  15.6 us
    all_gather x1, waiting for transfers between devices, merged(): gathered = jax.tree.map(lambda a: lax.all_gather(a, axis), part)  13.1 us
    all_to_all x1, starting transfers between devices, on_device(): lax.all_to_all(summed.reshape(ep_count, CAP, -1).astype(jnp.bfloat16), 'e...  10.4 us
    all_gather x1, waiting for transfers between devices, on_device(): lax.all_gather(hidden, 'kv', axis=1, tiled=True)  6.04 us
  transfers between devices with their start and end apart: 4, of which 3 were waited for; matrix products, arithmetic and copies ran while one was open for 5% of the time, Pallas kernels for 0%

commit v1 on v0

--- a/solution.py
+++ b/solution.py
@@ -175,7 +175,9 @@
         -1, out_width
     )
     summed = jnp.dot(
-        lax.all_gather(hidden, "kv", axis=1, tiled=True),
+        jnp.concatenate(
+            lax.all_to_all(jnp.stack([hidden] * lax.axis_size("kv")), "kv", 0, 0), axis=1
+        ),
         down_cols,
         preferred_element_type=jnp.float32,
     )

time: 285 us -> 305 us (1.070)
  blocking collectives: 137 us -> 29.7 us
  waiting for transfers between devices: 48.1 us -> 149 us
  starting transfers between devices: 26.1 us -> 36.2 us
  local copies, waits for them, and re-layouts: 16 us -> 25.4 us
  matrix products: 10.8 us -> 17.2 us
    all_to_all x0 -> x2, waiting for transfers between devices: none -> 129 us  [the longest x1 82.6 us: on_device(): lax.all_to_all(outgoing, 'ep', split_axis=0, concat_axis=0, tiled=True)]
    all_to_all x1 -> x0, blocking collectives: 102 us -> none  [on_device(): lax.all_to_all(outgoing, 'ep', split_axis=0, concat_axis=0, tiled=True)]
    all_to_all x0 -> x2, starting transfers between devices: none -> 26.5 us  [the longest x1 15.7 us: on_device(): lax.all_to_all(jnp.stack([hidden] * lax.axis_size('kv')), 'kv', 0, 0)]
    all_gather x1, waiting for transfers between devices: 13.1 us -> 0.01 us  [merged(): gathered = jax.tree.map(lambda a: lax.all_gather(a, axis), part)]
    all_to_all x1, starting transfers between devices: 15.6 us -> 4.85 us  [on_device(): lax.all_to_all(down_split, 'kv', split_axis=1, concat_axis=0, tiled=True)]
    all_to_all x1, waiting for transfers between devices: 28.9 us -> 19.9 us  [on_device(): lax.all_to_all(down_split, 'kv', split_axis=1, concat_axis=0, tiled=True)]
    all_gather x1 -> x0, waiting for transfers between devices: 6.04 us -> none  [on_device(): lax.all_gather(hidden, 'kv', axis=1, tiled=True)]
    all_to_all x1, starting transfers between devices: 10.4 us -> 4.79 us  [on_device(): lax.all_to_all(summed.reshape(ep_count, CAP, -1).astype(jnp.bfloat16), 'e...]
  transfers between devices with their start and end apart: 4 -> 5, of which waited for: 3 -> 3; matrix products, arithmetic and copies ran while one was open for 5% -> 10% of each run, Pallas kernels for 0% -> 0%
where the time goes in v1:
time: 305 us; the launch traced here: 304 us
  waiting for transfers between devices  149 us (49%)
  starting transfers between devices  36.2 us (12%)
  other arithmetic  30.8 us (10%)
  blocking collectives  29.7 us (10%)
  local copies, waits for them, and re-layouts  25.4 us (8%)
  matrix products  17.2 us (6%)
  between operations  15 us (5%)
    all_to_all x1, waiting for transfers between devices, on_device(): lax.all_to_all(outgoing, 'ep', split_axis=0, concat_axis=0, tiled=True)  82.6 us
    all_to_all x1, waiting for transfers between devices, on_device(): lax.all_to_all(jnp.stack([hidden] * lax.axis_size('kv')), 'kv', 0, 0)  46.3 us
    all_gather x2, blocking collectives, merged(): gathered = jax.tree.map(lambda a: lax.all_gather(a, axis), part)  29.7 us
    add x15, other arithmetic, combine_parts(): blend_first.reshape(row_count, head_count, -1) * factor_first[..., None]  23.9 us
    all_to_all x1, waiting for transfers between devices, on_device(): lax.all_to_all(down_split, 'kv', split_axis=1, concat_axis=0, tiled=True)  19.9 us
    all_to_all x1, starting transfers between devices, on_device(): lax.all_to_all(jnp.stack([hidden] * lax.axis_size('kv')), 'kv', 0, 0)  15.7 us
    all_to_all x1, starting transfers between devices, on_device(): lax.all_to_all(outgoing, 'ep', split_axis=0, concat_axis=0, tiled=True)  10.7 us
  transfers between devices with their start and end apart: 5, of which 3 were waited for; matrix products, arithmetic and copies ran while one was open for 10% of the time, Pallas kernels for 0%

profile of v1, /device:TPU:1, one launch (start us, length us, event | category | flops | bytes accessed | tf_op | source)
XLA Modules:
  0.0 303.7 jit_solution(1586962077159604792)
XLA Ops:
  7.2 0.8 copy.57
  8.7 0.8 convert_reduce_fusion
  9.5 4.2 %convolution_convert_fusion = bf16[512,4096]{1,0:T(8,128)(2,1)} fusion(bf16[32,4096]{1,0:T(8,128)(2,1)} %param.22, bf16[512,32]{0,1:T(8,128)(2,1)S(1)} %get-tuple-element.181), kind=kOutput, calls=%fused_computation.9 | convolution fusion | flops 136314880 | bytes 4489216 | tf_op jit(solution)/shard_map/dot_general | solution.py:162
  13.7 10.7 %all-to-all-start = ((bf16[32,16,4096]{2,1,0:T(8,128)(2,1)}), bf16[32,16,4096]{2,1,0:T(8,128)(2,1)}, u32[]{:S(2)}, u32[]{:S(2)}) async-start(bf16[32,16,4096]{2,1,0:T(8,128)(2,1)} %bitcast.133), calls=%async_computation | async-start | bytes 8388608 | tf_op jit(solution)/shard_map/all_to_all | solution.py:166
  25.7 0.2 fusion.50
  25.9 0.2 multiply_cosine_fusion
  26.4 0.9 copy.51
  27.3 1.2 reshape_squeeze.10
  28.6 0.7 bitcast_convert_fusion
  29.4 0.3 subtract_convert_fusion
  29.8 1.8 fusion.3
  31.6 0.8 fusion.9
  32.4 0.7 copy-done.1
  33.1 0.3 copy.55
  33.4 1.0 all_gather_reshape.11
  34.5 82.6 %all-to-all-done = bf16[32,16,4096]{2,1,0:T(8,128)(2,1)} async-done(((bf16[32,16,4096]{2,1,0:T(8,128)(2,1)}), bf16[32,16,4096]{2,1,0:T(8,128)(2,1)}, u32[]{:S(2)}, u32[]{:S(2)}) %all-to-all-start) | async-done | bytes 4194336 | tf_op jit(solution)/shard_map/all_to_all | solution.py:166
  117.1 3.5 %fusion.14 = f32[512,128]{1,0:T(8,128)S(1)} fusion(bf16[512,4096]{1,0:T(8,128)(2,1)} %bitcast.24, bf16[1,4096,128]{2,1,0:T(8,128)(2,1)S(1)} %copy-done), kind=kOutput, calls=%fused_computation.23 | convolution fusion | flops 536870912 | bytes 5505024 | tf_op jit(solution)/shard_map/dot_general | solution.py:169
  120.6 3.4 %fusion.12 = bf16[512,128]{1,0:T(8,128)(2,1)S(1)} fusion(bf16[512,4096]{1,0:T(8,128)(2,1)} %bitcast.24, bf16[1,4096,128]{2,1,0:T(8,128)(2,1)S(1)} %copy-done.4, f32[512,128]{1,0:T(8,128)S(1)} %fusion.14), kind=kOutput, calls=%fused_computation.20 | convolution fusion | flops 537264128 | bytes 5636096 | tf_op jit(solution)/shard_map/dot_general | solution.py:170
  124.1 1.8 stack.2
  125.8 15.7 %all-to-all-start.1 = ((bf16[16,512,128]{2,1,0:T(8,128)(2,1)}), bf16[16,512,128]{2,1,0:T(8,128)(2,1)S(1)}, u32[]{:S(2)}, u32[]{:S(2)}) async-start(bf16[16,512,128]{2,1,0:T(8,128)(2,1)} %stack.2), calls=%async_computation.1 | async-start | bytes 4194304 | tf_op jit(solution)/shard_map/all_to_all | solution.py:179
  141.6 1.5 copy.69
  143.0 1.3 copy.60
  144.4 46.3 %all-to-all-done.1 = bf16[16,512,128]{2,1,0:T(8,128)(2,1)S(1)} async-done(((bf16[16,512,128]{2,1,0:T(8,128)(2,1)}), bf16[16,512,128]{2,1,0:T(8,128)(2,1)S(1)}, u32[]{:S(2)}, u32[]{:S(2)}) %all-to-all-start.1) | async-done | bytes 2097184 | tf_op jit(solution)/shard_map/all_to_all | solution.py:179
  190.6 4.8 %all-to-all-start.2 = ((bf16[128,16,256]{2,0,1:T(8,128)(2,1)}), bf16[128,16,256]{2,0,1:T(8,128)(2,1)}, u32[]{:S(2)}, u32[]{:S(2)}) async-start(bf16[128,16,256]{2,0,1:T(8,128)(2,1)} %copy.60), calls=%async_computation.2 | async-start | bytes 2097152 | tf_op jit(solution)/shard_map/all_to_all | solution.py:174
  195.5 2.6 fusion.5
  198.1 2.7 copy.59
  200.8 2.8 dot_general.28
  203.6 19.9 %all-to-all-done.2 = bf16[128,16,256]{2,0,1:T(8,128)(2,1)} async-done(((bf16[128,16,256]{2,0,1:T(8,128)(2,1)}), bf16[128,16,256]{2,0,1:T(8,128)(2,1)}, u32[]{:S(2)}, u32[]{:S(2)}) %all-to-all-start.2) | async-done | bytes 1048608 | tf_op jit(solution)/shard_map/all_to_all | solution.py:174
  223.6 2.6 convolution_convert_fusion.1
  226.2 4.8 %all-to-all-start.3 = ((bf16[32,16,256]{2,1,0:T(8,128)(2,1)}), bf16[32,16,256]{2,1,0:T(8,128)(2,1)S(1)}, u32[]{:S(2)}, u32[]{:S(2)}) async-start(bf16[32,16,256]{2,1,0:T(8,128)(2,1)} %convolution_convert_fusion.1), calls=%async_computation.3 | async-start | bytes 524288 | tf_op jit(solution)/shard_map/all_to_all | solution.py:185
  231.0 14.8 %all_gather.9 = f32[16,64,16]{1,2,0:T(8,128)S(1)} all-gather(f32[1,64,16]{1,2,0:T(8,128)S(1)} %bitcast.142), channel_id=1, replica_groups=mesh['kv'=16,'ep'=32] {'kv'}, dimensions={0}, use_global_device_ids=true | all-gather | bytes 69632 | tf_op jit(solution)/shard_map/all_gather | solution.py:20
  245.8 14.8 %all_gather.10 = f32[16,64,16]{1,2,0:T(8,128)S(1)} all-gather(f32[1,64,16]{1,2,0:T(8,128)S(1)} %bitcast.143), channel_id=1, replica_groups=mesh['kv'=16,'ep'=32] {'kv'}, dimensions={0}, use_global_device_ids=true | all-gather | bytes 69632 | tf_op jit(solution)/shard_map/all_gather | solution.py:20
  260.7 0.9 convolution_convert_fusion.2
  261.5 1.1 slice_bitcast_fusion
  262.6 33.0 %while.19 = (s32[]{:T(128)}, f32[64,16]{0,1:T(8,128)S(1)}, f32[64,16]{0,1:T(8,128)S(1)}, f32[64,2048]{1,0:T(8,128)S(1)}, f32[16,64,16]{1,2,0:T(8,128)S(1)}, /*in...) while((s32[]{:T(128)}, f32[64,16]{0,1:T(8,128)S(1)}, ...), condition=%wide.region_4.5_spmd, body=%wide.region_3.4_spmd.sunk | while | flops 399365 | bytes 3727511 | solution.py:25
  263.2 1.6 fusion.62
  265.2 0.2 mul.309
  265.4 1.6 fusion.62
  267.4 0.2 mul.309
  267.6 1.6 fusion.62
  269.6 0.2 mul.309
  269.8 1.6 fusion.62
  271.8 0.2 mul.309
  272.0 1.6 fusion.62
  274.0 0.2 mul.309
  274.2 1.6 fusion.62
  276.2 0.2 mul.309
  276.4 1.6 fusion.62
  278.4 0.2 mul.309
  278.6 1.6 fusion.62
  280.6 0.2 mul.309
  280.8 1.6 fusion.62
  282.8 0.2 mul.309
  283.0 1.6 fusion.62
  285.0 0.2 mul.309
  285.2 1.6 fusion.62
  287.2 0.2 mul.309
  287.4 1.6 fusion.62
  289.4 0.2 mul.309
  289.6 1.6 fusion.62
  291.6 0.2 mul.309
  291.8 1.6 fusion.62
  294.0 1.6 fusion.62
  295.9 0.9 fusion.27
  (105 shorter events, 8.0 us)
Async XLA Ops:
  7.2 109.9 %copy-start = (bf16[1,4096,128]{2,1,0:T(8,128)(2,1)S(1)}, bf16[1,4096,128]{2,1,0:T(8,128)(2,1)}, u32[]{:S(2)}) copy-start(bf16[1,4096,128]{2,1,0:T(8,128)(2,1)} %param.25) | copy-start | bytes 3145732
  13.7 11.6 %copy-start.5 = (s32[1,64]{1,0:T(1,128)S(1)}, s32[1,64]{1,0:T(1,128)}, u32[]{:S(2)}) copy-start(s32[1,64]{1,0:T(1,128)} %param.20) | copy-start | bytes 772
  13.7 11.9 %copy-start.3 = (bf16[1,64,2048]{2,1,0:T(8,128)(2,1)S(1)}, bf16[1,64,2048]{2,1,0:T(8,128)(2,1)}, u32[]{:S(2)}) copy-start(bf16[1,64,2048]{2,1,0:T(8,128)(2,1)} %param.15) | copy-start | bytes 786436
  13.7 103.4 %all-to-all-start = ((bf16[32,16,4096]{2,1,0:T(8,128)(2,1)}), bf16[32,16,4096]{2,1,0:T(8,128)(2,1)}, u32[]{:S(2)}, u32[]{:S(2)}) async-start(bf16[32,16,4096]{2,1,0:T(8,128)(2,1)} %bitcast.133), calls=%async_computation | async-start | bytes 8388608 | tf_op jit(solution)/shard_map/all_to_all | solution.py:166
  24.4 1.8 copy-start.2
  24.4 237.1 %all-gather.2.cloned.1.call-start = ((), (), s32[]{:S(2)}) async-start(), calls=%async_computation.4 | async-start | bytes 8912896 | tf_op jit(solution)/shard_map/all_gather | solution.py:20
  31.6 1.5 copy-start.1
  117.1 3.5 %copy-start.4 = (bf16[1,4096,128]{2,1,0:T(8,128)(2,1)S(1)}, bf16[1,4096,128]{2,1,0:T(8,128)(2,1)}, u32[]{:S(2)}) copy-start(bf16[1,4096,128]{2,1,0:T(8,128)(2,1)} %param.26) | copy-start | bytes 3145732
  125.8 64.8 %all-to-all-start.1 = ((bf16[16,512,128]{2,1,0:T(8,128)(2,1)}), bf16[16,512,128]{2,1,0:T(8,128)(2,1)S(1)}, u32[]{:S(2)}, u32[]{:S(2)}) async-start(bf16[16,512,128]{2,1,0:T(8,128)(2,1)} %stack.2), calls=%async_computation.1 | async-start | bytes 4194304 | tf_op jit(solution)/shard_map/all_to_all | solution.py:179
  190.6 32.9 %all-to-all-start.2 = ((bf16[128,16,256]{2,0,1:T(8,128)(2,1)}), bf16[128,16,256]{2,0,1:T(8,128)(2,1)}, u32[]{:S(2)}, u32[]{:S(2)}) async-start(bf16[128,16,256]{2,0,1:T(8,128)(2,1)} %copy.60), calls=%async_computation.2 | async-start | bytes 2097152 | tf_op jit(solution)/shard_map/all_to_all | solution.py:174
  226.2 34.5 %all-to-all-start.3 = ((bf16[32,16,256]{2,1,0:T(8,128)(2,1)}), bf16[32,16,256]{2,1,0:T(8,128)(2,1)S(1)}, u32[]{:S(2)}, u32[]{:S(2)}) async-start(bf16[32,16,256]{2,1,0:T(8,128)(2,1)} %convolution_convert_fusion.1), calls=%async_computation.3 | async-start | bytes 524288 | tf_op jit(solution)/shard_map/all_to_all | solution.py:185
Sparse Core Ops, SparseCore 0:
  34.6 64.3 all-gather.1
